TPU v7x, 32 devices: a whole 2x2x4 slice. The times are simulated.
32 devices in a mesh: seq: 16 (over z, x, core), tp: 2 (over y).
Axes of the slice: x: 2, y: 2, z: 4, core: 2. Of those that a mesh axis runs over, the one named last changes fastest.
Arguments:
- tokens: bfloat16 [8192, 5376], P(('seq', 'tp')), may hold values from -6 to 6
- norm_gain: float32 [5376], replicated, may hold values from 0.5 to 1.5
- w_query: bfloat16 [5376, 2048], P(None, 'tp'), may hold values from -0.078125 to 0.078125
- key_value_weight: bfloat16 [5376, 2048], P(None, 'tp'), may hold values from -0.078125 to 0.078125
- query_gain: float32 [128], replicated, may hold values from 0.5 to 7
- key_gain: float32 [128], replicated, may hold values from 0.5 to 7
- lengths: int32 [8], replicated, may hold values from 1 to 4096, as said below
- segment_ids: int32 [8192], P('seq'), may hold values from 0 to 7, as said below
- req_counts: int32 [8], replicated, may hold values from 8 to 16, as said below
- req_slots: int32 [128], replicated, may hold values from 0 to 131071, as said below
Outputs:
- attended: bfloat16 [8192, 2048], P('seq', 'tp')
- cache: bfloat16 [131072, 2048], P('seq', 'tp')
Inputs may be any that keep to these rules, and one draw needn't show every extreme that they name: lengths sum to 8192; the longest is exactly 4096. Prompts lie in order: prompt p covers lengths[p] consecutive tokens, so segment_ids never falls. `req_counts`: the requests of prompt p follow those of prompts before it; entries past all requests are unused. `req_slots`: the cache rows of different requests never intersect and lie within the cache; unused entries are 0.
All inputs are finite; a program needn't handle non-finite values.
Results may differ from a plain program's by a relative error of at most 0.005.
The roundings to bfloat16 on the way count: a program that leaves them out, or rounds other values in their place, can miss the bound.
Values may be sent and summed in bfloat16 or wider, within the bound.
No kernel may reach another device: no remote copies, remote signals or barrier semaphores. Data moves between devices by JAX's collectives and lax.ppermute only.
A program may use at most 192 MiB of HBM per device.

v0:
```python
import math
import jax
import jax.numpy as jnp
from jax import lax
from jax.sharding import PartitionSpec as P

CACHE_DEV = 8192
rope_base = 1000000.0
query_scalar = 168.0
epsilon = 1e-06


def rms_scale(values, gains):
    return values * lax.rsqrt(jnp.mean(values * values, axis=-1, keepdims=True) + epsilon) * gains


def rope_table(positions, head_width):
    half_width = head_width // 2
    frequency = jnp.exp(
        jnp.arange(half_width, dtype=jnp.float32) * (-2.0 * math.log(rope_base) / head_width)
    )
    angles = positions.astype(jnp.float32)[:, None] * frequency[None, :]
    return (jnp.cos(angles), jnp.sin(angles))


def rotate_pairs(values, cosine, sine_table):
    half_width = values.shape[-1] // 2
    front_half = values[..., :half_width]
    back_half = values[..., half_width:]
    cos_part = cosine[:, None, :]
    sin_part = sine_table[:, None, :]
    return jnp.concatenate(
        [
            front_half * cos_part - back_half * sin_part,
            back_half * cos_part + front_half * sin_part,
        ],
        axis=-1,
    )


def project(tokens, norm_gain, w_query, key_value_weight, query_gain, key_gain, positions):
    token_count = tokens.shape[0]
    head_width = query_gain.shape[0]
    as_float = tokens.astype(jnp.float32)
    normed = rms_scale(as_float, norm_gain).astype(jnp.bfloat16)
    query_raw = jnp.dot(normed, w_query, preferred_element_type=jnp.float32)
    keyval_raw = jnp.dot(normed, key_value_weight, preferred_element_type=jnp.float32)
    cosine, sine_table = rope_table(positions, head_width)
    query_rows = rotate_pairs(
        rms_scale(query_raw.reshape(token_count, -1, head_width), query_gain), cosine, sine_table
    ) * query_scalar ** (-0.5)
    split_kv = keyval_raw.reshape(token_count, -1, 2, head_width)
    keys = rotate_pairs(rms_scale(split_kv[:, :, 0], key_gain), cosine, sine_table)
    key_value_rows = (
        jnp.stack([keys, split_kv[:, :, 1]], axis=2).reshape(token_count, -1).astype(jnp.bfloat16)
    )
    return (query_rows.reshape(token_count, -1).astype(jnp.bfloat16), key_value_rows)


def prompt_starts(segment_ids, lengths):
    starts = jnp.cumsum(lengths) - lengths
    prompt_ids = jnp.arange(lengths.shape[0], dtype=jnp.int32)
    chosen = jnp.where(segment_ids[:, None] == prompt_ids[None, :], starts[None, :], jnp.int32(0))
    return jnp.sum(chosen, axis=1)


def sources(cache_index, lengths, req_counts, req_slots):
    starts = jnp.cumsum(lengths) - lengths
    prompt_ids = jnp.arange(lengths.shape[0], dtype=jnp.int32)
    request_ids = jnp.arange(req_slots.shape[0], dtype=jnp.int32)
    request_ends = jnp.cumsum(req_counts)
    owner_prompt = jnp.sum(
        (request_ends[None, :] <= request_ids[:, None]).astype(jnp.int32), axis=1
    )
    matches = owner_prompt[:, None] == prompt_ids[None, :]
    request_length = jnp.sum(jnp.where(matches, lengths[None, :], jnp.int32(0)), axis=1)
    request_start = jnp.sum(jnp.where(matches, starts[None, :], jnp.int32(0)), axis=1)
    inside = (cache_index[:, None] >= req_slots[None, :]) & (
        cache_index[:, None] < req_slots[None, :] + request_length[None, :]
    )
    offsets = request_start[None, :] + cache_index[:, None] - req_slots[None, :]
    source_row = jnp.sum(jnp.where(inside, offsets, jnp.int32(0)), axis=1)
    source_live = jnp.max(inside.astype(jnp.int32), axis=1) > 0
    return (source_row, source_live)


def on_device(
    tokens,
    norm_gain,
    w_query,
    key_value_weight,
    query_gain,
    key_gain,
    lengths,
    segment_ids,
    req_counts,
    req_slots,
):
    gathered = lax.all_gather(tokens, "tp", axis=0, tiled=True)
    row_count = gathered.shape[0]
    seq_rank = lax.axis_index("seq")
    first_row = seq_rank * row_count
    query_index = first_row + jnp.arange(row_count, dtype=jnp.int32)
    positions = query_index - prompt_starts(segment_ids, lengths)
    query_rows, key_value_rows = project(
        gathered, norm_gain, w_query, key_value_weight, query_gain, key_gain, positions
    )
    head_width = query_gain.shape[0]
    kv_heads = key_value_rows.shape[1] // (2 * head_width)
    query_heads = query_rows.reshape(row_count, kv_heads, 2, head_width)
    cache_index = seq_rank * CACHE_DEV + jnp.arange(CACHE_DEV, dtype=jnp.int32)
    source_row, source_live = sources(cache_index, lengths, req_counts, req_slots)

    def attend_block(state_now, key_block, seg_block, block_start):
        maxima, totals, running = state_now
        key_count = key_block.shape[0]
        grouped_heads = key_block.reshape(key_count, kv_heads, 2, head_width)
        key_part = grouped_heads[:, :, 0]
        value_part = grouped_heads[:, :, 1]
        key_index = block_start + jnp.arange(key_count, dtype=jnp.int32)
        allowed = (seg_block[None, :] == segment_ids[:, None]) & (
            key_index[None, :] <= query_index[:, None]
        )
        scores = jnp.einsum(
            "qgrd,kgd->grqk", query_heads, key_part, preferred_element_type=jnp.float32
        )
        new_maxima = jnp.maximum(maxima, jnp.max(jnp.where(allowed, scores, -1e30), axis=-1))
        factor = jnp.exp(maxima - new_maxima)
        exp_scores = jnp.where(allowed, jnp.exp(scores - new_maxima[..., None]), 0.0)
        totals = totals * factor + jnp.sum(exp_scores, axis=-1)
        weighted = jnp.einsum(
            "grqk,kgd->qgrd",
            exp_scores.astype(jnp.bfloat16),
            value_part,
            preferred_element_type=jnp.float32,
        )
        running = running * jnp.transpose(factor, (2, 0, 1))[..., None] + weighted
        return (new_maxima, totals, running)

    def attend_piece(state_now, key_block, seg_block, block_start):
        return attend_block(state_now, key_block, seg_block, block_start)

    initial = (
        jnp.full((kv_heads, 2, row_count), -1e30, jnp.float32),
        jnp.zeros((kv_heads, 2, row_count), jnp.float32),
        jnp.zeros((row_count, kv_heads, 2, head_width), jnp.float32),
    )
    key_block = lax.all_gather(key_value_rows, "seq", axis=0, tiled=True)
    seg_block = lax.all_gather(segment_ids, "seq", axis=0, tiled=True)
    key_count = key_block.shape[0]
    block_span = 512

    def inner(counter, current):
        offset = counter * block_span
        key_slice = lax.dynamic_slice_in_dim(key_block, offset, block_span, 0)
        seg_slice = lax.dynamic_slice_in_dim(seg_block, offset, block_span, 0)
        return attend_piece(current, key_slice, seg_slice, offset)

    final_state = lax.fori_loop(0, key_count // block_span, inner, initial)
    every_row = lax.all_gather(key_value_rows, "seq", axis=0, tiled=True)
    picked = jnp.take(every_row, source_row, axis=0)
    cache = jnp.where(source_live[:, None], picked, jnp.zeros_like(picked))
    maxima, totals, running = final_state
    attended = (
        (running / jnp.transpose(totals, (2, 0, 1))[..., None])
        .reshape(row_count, -1)
        .astype(jnp.bfloat16)
    )
    return (attended, cache)


def solution(mesh):
    placed = (
        P(("seq", "tp"), None),
        P(),
        P(None, "tp"),
        P(None, "tp"),
        P(),
        P(),
        P(),
        P("seq"),
        P(),
        P(),
    )
    return jax.shard_map(
        on_device,
        mesh=mesh,
        in_specs=placed,
        out_specs=(P("seq", "tp"), P("seq", "tp")),
        check_vma=False,
    )
```

profile of v0, /device:TPU:0, one launch (start us, length us, event | category | flops | bytes accessed | tf_op | source)
XLA Modules:
  0.0 477.4 jit_solution(2000407036407505934)
XLA Ops:
  11.2 72.6 %all-gather.4.cloned.1.call-done = bf16[512,5376]{1,0:T(8,128)(2,1)} async-done(((bf16[256,5376]{1,0:T(8,128)(2,1)}), bf16[512,5376]{1,0:T(8,128)(2,1)}) %all-gather.4.cloned.1.call-update) | async-done | bytes 5505040 | tf_op jit(solution)/shard_map/all_gather | solution.py:99
  83.8 3.9 fusion.19
  88.0 8.7 %fusion.24 = f32[512,1024]{1,0:T(8,128)S(1)} fusion(bf16[5376,1024]{1,0:T(8,128)(2,1)} %param.15, bf16[512,5376]{1,0:T(8,128)(2,1)S(1)} %copy-done.1, f32[5376]{0:T(1024)S(1)} %copy-done.7, f32[512]{0:T(512)S(1)} %add_rsqrt_fusion.2), kind=kOutput, calls=%fused_computation.46 | convolution fusion | flops 5648154624 | bytes 18635776 | tf_op jit(solution)/shard_map/dot_general | solution.py:47
  96.7 2.8 reshape.208
  99.5 2.3 slice.45
  101.8 2.7 slice.48
  109.2 22.1 %all-gather = s32[16,1,512]{2,1,0:T(1,128)S(1)} all-gather(s32[1,1,512]{2,1,0:T(1,128)S(1)} %bitcast.91), channel_id=1, replica_groups=mesh['seq'=16,'tp'=2] {'seq'}, dimensions={0}, use_global_device_ids=true | all-gather | bytes 34816 | tf_op jit(solution)/shard_map/all_gather | solution.py:149
  131.3 3.7 convert_reduce_fusion
  135.1 10.4 %convolution_bitcast_fusion = f32[64,8,8,128]{3,1,2,0:T(8,128)S(1)} fusion(bf16[5376,1024]{1,0:T(8,128)(2,1)} %param.14, bf16[512,5376]{1,0:T(8,128)(2,1)} %all-gather.4.cloned.1.call-done, f32[5376]{0:T(1024)S(1)} %copy-done.7, f32[512]{0:T(512)S(1)} %add_rsqrt_fusion.2), kind=kOutput, calls=%fused_computation.45 | convolution fusion | flops 5648154624 | bytes 18635776 | tf_op jit(solution)/shard_map/dot_general | solution.py:46
  153.0 83.2 %all-gather.6.cloned.1.call-done = bf16[8192,1024]{1,0:T(8,128)(2,1)} async-done(((bf16[512,1024]{1,0:T(8,128)(2,1)}), bf16[8192,1024]{1,0:T(8,128)(2,1)}) %all-gather.6.cloned.1.call-update) | async-done | bytes 16777232 | tf_op jit(solution)/shard_map/all_gather | solution.py:148
  236.1 169.9 %while.18 = (s32[]{:T(128)}, f32[4,2,512]{2,1,0:T(2,128)S(1)}, f32[4,2,512]{2,1,0:T(2,128)S(1)}, f32[512,4,2,128]{0,3,2,1:T(8,128)S(1)}, s32[8192]{0:T(1024)S(1)...) while((s32[]{:T(128)}, f32[4,2,512]{2,1,0:T(2,128)S(1)}, ...), condition=%wide.region_8.9_spmd.clone, body=%wide.region_5.8_spmd.clone.sunk | while | flops 1092903936 | bytes 36978892 | solution.py:159
  236.5 2.3 constant_dynamic-slice_fusion.2
  240.3 2.7 fusion.38
  247.1 2.3 constant_dynamic-slice_fusion.2
  250.9 2.7 fusion.38
  257.7 2.3 constant_dynamic-slice_fusion.2
  261.5 2.7 fusion.38
  272.1 2.7 fusion.38
  282.8 2.7 fusion.38
  293.4 2.7 fusion.38
  304.0 2.7 fusion.38
  314.6 2.7 fusion.38
  325.2 2.7 fusion.38
  335.9 2.7 fusion.38
  346.5 2.7 fusion.38
  357.1 2.7 fusion.38
  367.7 2.7 fusion.38
  378.3 2.7 fusion.38
  388.9 2.7 fusion.38
  399.6 2.7 fusion.38
  407.6 48.4 %gather_fusion = bf16[8192,1024]{1,0:T(8,128)(2,1)} fusion(bf16[8192,1024]{1,0:T(8,128)(2,1)} %get-tuple-element.382, s32[8192]{0:T(1024)S(1)} %broadcast_clamp_fusion), kind=kCustom, calls=%fused_computation | custom fusion | bytes 33587200 | tf_op jit(solution)/shard_map/jit(_take)/gather | solution.py:161
  456.0 14.6 %select_select_fusion = bf16[8192,1024]{1,0:T(8,128)(2,1)} fusion(bf16[8192,1024]{1,0:T(8,128)(2,1)} %gather_fusion, pred[8192]{0:T(1024)(128)(4,1)S(1)} %get-tuple-element.271, pred[8192]{0:T(1024)(128)(4,1)S(1)} %get-tuple-element.272), kind=kLoop, calls=%fused_computation.29 | loop fusion | flops 16777216 | bytes 33570816 | tf_op jit(solution)/shard_map/jit(_where)/select_n | solution.py:162
  (217 shorter events, 137.2 us)
Async XLA Ops:
  7.2 80.5 %copy-start.7 = (f32[5376]{0:T(1024)S(1)}, f32[5376]{0:T(1024)}, u32[]{:S(2)}) copy-start(f32[5376]{0:T(1024)} %param.13) | copy-start | bytes 64516
  7.2 76.6 %all-gather.4.cloned.1.call-start = ((), (), s32[]{:S(2)}) async-start(), calls=%async_computation | async-start | bytes 8257536 | tf_op jit(solution)/shard_map/all_gather | solution.py:99
  7.9 228.2 %all-gather.6.cloned.1.call-start = ((), (), s32[]{:S(2)}) async-start(), calls=%async_computation.1 | async-start | bytes 17825792 | tf_op jit(solution)/shard_map/all_gather | solution.py:148
  83.8 4.2 copy-start.1
  99.5 5.5 %copy-start.3 = (f32[128]{0:T(128)S(1)}, f32[128]{0:T(128)}, u32[]{:S(2)}) copy-start(f32[128]{0:T(128)} %param.17) | copy-start | bytes 1540
  105.7 3.2 copy-start.8
  105.7 3.4 copy-start.6
  105.7 3.5 copy-start.4
  105.7 3.5 copy-start.2
  145.5 2.7 copy-start.5
  146.0 1.3 copy-start
Sparse Core Ops, SparseCore 0:
  9.5 74.2 all-gather.3
  108.9 127.1 all-gather.5
where the time goes:
time: 479 us; the launch traced here: 477 us
  waiting for transfers between devices  156 us (33%)
  local copies, waits for them, and re-layouts  125 us (26%)
  matrix products  97.2 us (20%)
  other arithmetic  61 us (13%)
  blocking collectives  22.1 us (5%)
  between operations  14.4 us (3%)
    all_gather x1, waiting for transfers between devices, on_device(): key_block = lax.all_gather(key_value_rows, 'seq', axis=0, tiled=True)  83.2 us
    all_gather x1, waiting for transfers between devices, on_device(): gathered = lax.all_gather(tokens, 'tp', axis=0, tiled=True)  72.6 us
    dynamic_slice x32, local copies, waits for them, and re-layouts, inner(): key_slice = lax.dynamic_slice_in_dim(key_block, offset, block_span, 0)  60.2 us
    gather x1, local copies, waits for them, and re-layouts, on_device(): picked = jnp.take(every_row, source_row, axis=0)  48.4 us
    dot_general x16, matrix products, attend_block(): jnp.einsum('qgrd,kgd->grqk', query_heads, key_part, preferred_element_typ...  42.8 us
    dot_general x16, matrix products, attend_block(): jnp.einsum('grqk,kgd->qgrd', exp_scores.astype(jnp.bfloat16), value_part,...  35.3 us
    reduce_sum x16, other arithmetic, attend_block(): totals = totals * factor + jnp.sum(exp_scores, axis=-1)  23.6 us
    all_gather x1, blocking collectives, on_device(): seg_block = lax.all_gather(segment_ids, 'seq', axis=0, tiled=True)  22.1 us
  transfers between devices with their start and end apart: 2, of which 2 were waited for; matrix products, arithmetic and copies ran while one was open for 5% of the time, Pallas kernels for 0%

commit v1 on v0

--- a/solution.py
+++ b/solution.py
@@ -96,7 +96,14 @@
     req_counts,
     req_slots,
 ):
-    gathered = lax.all_gather(tokens, "tp", axis=0, tiled=True)
+    ways, here, step = (lax.axis_size("tp"), lax.axis_index("tp"), tokens.shape[0])
+    line, have = (tokens, 1)
+    while have < ways:
+        line = jnp.concatenate(
+            [line, lax.ppermute(line, "tp", [(d, (d - have) % ways) for d in range(ways)])], axis=0
+        )
+        have = 2 * have
+    gathered = jnp.roll(line, here * step, axis=0)
     row_count = gathered.shape[0]
     seq_rank = lax.axis_index("seq")
     first_row = seq_rank * row_count

time: 479 us -> 467 us (0.975)
  waiting for transfers between devices: 156 us -> 141 us
    all_gather x1 -> x0, waiting for transfers between devices: 72.6 us -> none  [on_device(): gathered = lax.all_gather(tokens, 'tp', axis=0, tiled=True)]
    ppermute x0 -> x1, waiting for transfers between devices: none -> 56.6 us  [on_device(): lax.ppermute(line, 'tp', [(d, (d - have) % ways) for d in range(ways)])]
where the time goes in v1:
time: 467 us; the launch traced here: 465 us
  waiting for transfers between devices  141 us (30%)
  local copies, waits for them, and re-layouts  124 us (27%)
  matrix products  95.8 us (21%)
  other arithmetic  63.2 us (14%)
  blocking collectives  22.5 us (5%)
  between operations  14.4 us (3%)
    all_gather x1, waiting for transfers between devices, on_device(): key_block = lax.all_gather(key_value_rows, 'seq', axis=0, tiled=True)  84.3 us
    dynamic_slice x32, local copies, waits for them, and re-layouts, inner(): key_slice = lax.dynamic_slice_in_dim(key_block, offset, block_span, 0)  60.2 us
    ppermute x1, waiting for transfers between devices, on_device(): lax.ppermute(line, 'tp', [(d, (d - have) % ways) for d in range(ways)])  56.6 us
    gather x1, local copies, waits for them, and re-layouts, on_device(): picked = jnp.take(every_row, source_row, axis=0)  48.4 us
    dot_general x16, matrix products, attend_block(): jnp.einsum('qgrd,kgd->grqk', query_heads, key_part, preferred_element_typ...  42.8 us
    dot_general x16, matrix products, attend_block(): jnp.einsum('grqk,kgd->qgrd', exp_scores.astype(jnp.bfloat16), value_part,...  35.3 us
    reduce_sum x16, other arithmetic, attend_block(): totals = totals * factor + jnp.sum(exp_scores, axis=-1)  23.6 us
    all_gather x1, blocking collectives, on_device(): seg_block = lax.all_gather(segment_ids, 'seq', axis=0, tiled=True)  22.5 us
  transfers between devices with their start and end apart: 2, of which 2 were waited for; matrix products, arithmetic and copies ran while one was open for 5% of the time, Pallas kernels for 0%

profile of v1, /device:TPU:0, one launch (start us, length us, event | category | flops | bytes accessed | tf_op | source)
XLA Modules:
  0.0 465.3 jit_solution(6192074083204751233)
XLA Ops:
  7.2 3.0 collective-permute-start
  13.5 56.6 %collective-permute-done = bf16[256,5376]{1,0:T(8,128)(2,1)S(1)} collective-permute-done((bf16[256,5376]{1,0:T(8,128)(2,1)}, bf16[256,5376]{1,0:T(8,128)(2,1)S(1)}, u32[]{:S(2)}, u32[]{:S(2)}) %collective-permute-start) | collective-permute-done | bytes 2752544 | tf_op jit(solution)/shard_map/ppermute | solution.py:103
  70.1 6.0 %fusion.19 = (f32[512]{0:T(512)S(1)}, bf16[512,5376]{1,0:T(8,128)(2,1)S(1)}) fusion(s32[]{:T(128)S(6)} %select_n.76, bf16[256,5376]{1,0:T(8,128)(2,1)S(1)} %collective-permute-done, bf16[256,5376]{1,0:T(8,128)(2,1)} %param.12), kind=kLoop, calls=%fused_computation.32 | loop fusion | flops 30277120 | bytes 11012100 | tf_op jit(solution)/shard_map/reduce_sum | solution.py:14
  76.2 2.4 copy-done.1
  78.6 7.3 %fusion.27 = f32[512,1024]{1,0:T(8,128)} fusion(bf16[5376,1024]{1,0:T(8,128)(2,1)S(1)} %copy-done.7, bf16[512,5376]{1,0:T(8,128)(2,1)S(1)} %get-tuple-element.262, f32[5376]{0:T(1024)S(1)} %copy-done.8, f32[512]{0:T(512)S(1)} %add_rsqrt_fusion.2), kind=kOutput, calls=%fused_computation.53 | convolution fusion | flops 5648154624 | bytes 18635776 | tf_op jit(solution)/shard_map/dot_general | solution.py:47
  86.0 3.0 reshape.208
  95.6 22.5 %all-gather = s32[16,1,512]{2,1,0:T(1,128)S(1)} all-gather(s32[1,1,512]{2,1,0:T(1,128)S(1)} %bitcast.91), channel_id=1, replica_groups=mesh['seq'=16,'tp'=2] {'seq'}, dimensions={0}, use_global_device_ids=true | all-gather | bytes 34816 | tf_op jit(solution)/shard_map/all_gather | solution.py:156
  118.1 3.7 convert_reduce_fusion
  121.9 10.4 %convolution_bitcast_fusion = f32[64,8,8,128]{3,1,2,0:T(8,128)S(1)} fusion(bf16[5376,1024]{1,0:T(8,128)(2,1)} %param.14, bf16[512,5376]{1,0:T(8,128)(2,1)} %copy-done.1, f32[5376]{0:T(1024)S(1)} %copy-done.8, f32[512]{0:T(512)S(1)} %add_rsqrt_fusion.2), kind=kOutput, calls=%fused_computation.52 | convolution fusion | flops 5648154624 | bytes 18635776 | tf_op jit(solution)/shard_map/dot_general | solution.py:46
  139.8 84.3 %all-gather.3.cloned.1.call-done = bf16[8192,1024]{1,0:T(8,128)(2,1)} async-done(((bf16[512,1024]{1,0:T(8,128)(2,1)}), bf16[8192,1024]{1,0:T(8,128)(2,1)}) %all-gather.3.cloned.1.call-update) | async-done | bytes 16777232 | tf_op jit(solution)/shard_map/all_gather | solution.py:155
  224.0 169.9 %while.18 = (s32[]{:T(128)}, f32[4,2,512]{2,1,0:T(2,128)S(1)}, f32[4,2,512]{2,1,0:T(2,128)S(1)}, f32[512,4,2,128]{0,3,2,1:T(8,128)S(1)}, s32[8192]{0:T(1024)S(1)...) while((s32[]{:T(128)}, f32[4,2,512]{2,1,0:T(2,128)S(1)}, ...), condition=%wide.region_8.9_spmd.clone, body=%wide.region_5.8_spmd.clone.sunk | while | flops 1092903936 | bytes 36978892 | solution.py:166
  224.4 2.3 constant_dynamic-slice_fusion.2
  228.2 2.7 fusion.42
  235.0 2.3 constant_dynamic-slice_fusion.2
  238.8 2.7 fusion.42
  249.4 2.7 fusion.42
  256.2 2.3 constant_dynamic-slice_fusion.2
  260.0 2.7 fusion.42
  270.6 2.7 fusion.42
  281.2 2.7 fusion.42
  291.9 2.7 fusion.42
  302.5 2.7 fusion.42
  313.1 2.7 fusion.42
  323.7 2.7 fusion.42
  334.3 2.7 fusion.42
  345.0 2.7 fusion.42
  355.6 2.7 fusion.42
  366.2 2.7 fusion.42
  376.8 2.7 fusion.42
  387.4 2.7 fusion.42
  395.5 48.4 %gather_fusion = bf16[8192,1024]{1,0:T(8,128)(2,1)} fusion(bf16[8192,1024]{1,0:T(8,128)(2,1)} %get-tuple-element.383, s32[8192]{0:T(1024)S(1)} %broadcast_clamp_fusion), kind=kCustom, calls=%fused_computation | custom fusion | bytes 33587200 | tf_op jit(solution)/shard_map/jit(_take)/gather | solution.py:168
  443.9 14.6 %select_select_fusion = bf16[8192,1024]{1,0:T(8,128)(2,1)} fusion(bf16[8192,1024]{1,0:T(8,128)(2,1)} %gather_fusion, pred[8192]{0:T(1024)(128)(4,1)S(1)} %get-tuple-element.273, pred[8192]{0:T(1024)(128)(4,1)S(1)} %get-tuple-element.274), kind=kLoop, calls=%fused_computation.29 | loop fusion | flops 16777216 | bytes 33570816 | tf_op jit(solution)/shard_map/jit(_where)/select_n | solution.py:169
  (218 shorter events, 138.0 us)
Async XLA Ops:
  7.2 216.9 %all-gather.3.cloned.1.call-start = ((), (), s32[]{:S(2)}) async-start(), calls=%async_computation | async-start | bytes 17825792 | tf_op jit(solution)/shard_map/all_gather | solution.py:155
  7.2 62.9 %collective-permute-start = (bf16[256,5376]{1,0:T(8,128)(2,1)}, bf16[256,5376]{1,0:T(8,128)(2,1)S(1)}, u32[]{:S(2)}, u32[]{:S(2)}) collective-permute-start(bf16[256,5376]{1,0:T(8,128)(2,1)} %param.12), channel_id=1, source_target_pairs={{0,1},{1,0},{2,3},{3,2},{4,5},{5,4},{6,7},{7,6},{8,9},{9,8},{10,11... | collective-permute-start | bytes 8257544 | tf_op jit(solution)/shard_map/ppermute | solution.py:103
  12.5 66.1 %copy-start.8 = (f32[5376]{0:T(1024)S(1)}, f32[5376]{0:T(1024)}, u32[]{:S(2)}) copy-start(f32[5376]{0:T(1024)} %param.13) | copy-start | bytes 64516
  13.5 65.1 %copy-start.7 = (bf16[5376,1024]{1,0:T(8,128)(2,1)S(1)}, bf16[5376,1024]{1,0:T(8,128)(2,1)}, u32[]{:S(2)}) copy-start(bf16[5376,1024]{1,0:T(8,128)(2,1)} %param.15) | copy-start | bytes 33030148
  76.2 2.4 copy-start.1
  86.0 5.3 %copy-start.3 = (f32[128]{0:T(128)S(1)}, f32[128]{0:T(128)}, u32[]{:S(2)}) copy-start(f32[128]{0:T(128)} %param.17) | copy-start | bytes 1540
  91.6 3.6 copy-start.9
  91.7 3.9 copy-start.6
  91.7 3.9 copy-start.4
  91.7 3.9 copy-start.2
  132.3 2.7 copy-start.5
  132.8 1.3 copy-start
Sparse Core Ops, SparseCore 0:
  95.3 128.6 all-gather.2
